TPU v7x, 512 devices: a whole 4x8x8 slice. The times are simulated.
512 devices in a mesh: ctx: 128 (over y, z, core), tp: 4 (over x).
Axes of the slice: x: 4, y: 8, z: 8, core: 2. Of those that a mesh axis runs over, the one named last changes fastest.
Arguments:
- outer_gate: bfloat16 [32768, 2048], P('ctx', 'tp'), may hold values from -6 to 6
- inner_gate: bfloat16 [32768, 2048], P('ctx', 'tp'), may hold values from -6 to 6
- stream: bfloat16 [32768, 2048], P('ctx', 'tp'), may hold values from -6 to 6
- filters: bfloat16 [128, 128], P('tp'), may hold values from -1 to 1
- query_rows: bfloat16 [32768, 2048], P('ctx', 'tp'), may hold values from -49 to 49
- key_rows: bfloat16 [32768, 2048], P('ctx', 'tp'), may hold values from -4 to 4
Outputs:
- mixed: bfloat16 [32768, 2048], P('ctx', 'tp')
- attended: bfloat16 [32768, 2048], P('ctx', 'tp')
All inputs are finite; a program needn't handle non-finite values.
Results may differ from a plain program's by a relative error of at most 0.007.
Values may be sent and summed in bfloat16 or wider, within the bound.
No kernel may reach another device: no remote copies, remote signals or barrier semaphores. Data moves between devices by JAX's collectives and lax.ppermute only.
A program may use at most 64 MiB of HBM per device.

v0:
```python
import functools
import math

import jax
import jax.numpy as jnp
from jax import lax
from jax.sharding import Mesh, NamedSharding
from jax.sharding import PartitionSpec as P

HEAD_DIM = 128
LENGTH = 8192
CORES = 2
WINDOW_SHARDS = 8

NEGATIVE = -1e30
CTX_AXES = ("row", "col", "core")


def passed_along(block, axis, size, distance):
    route = [(i - distance, i) for i in range(size) if i - distance >= 0]
    return lax.ppermute(block, axis, route)


def toeplitz_taps(filters, offset):
    groups, kernel = filters.shape
    flipped = filters[:, ::-1]
    zeros = jnp.zeros_like(flipped)
    pieces = [flipped, zeros] if offset == 0 else [zeros, flipped]
    lags = jnp.concatenate(pieces, axis=1)
    flat = jnp.tile(lags, (1, kernel))[:, : kernel * (2 * kernel - 1)]
    return flat.reshape(groups, kernel, 2 * kernel - 1)[:, :, kernel - 1 : 2 * kernel - 1]


def apply_blocks(matrix, blocks):
    return jnp.einsum("gts,bsgc->btgc", matrix, blocks, preferred_element_type=jnp.float32)


def body(outer_gate, inner_gate, stream, filters, query_rows, key_rows, *, rows, half):
    row_count, channels = outer_gate.shape
    groups, kernel = filters.shape
    group_size = channels // groups
    seq_span = 2 * half
    ctx_size = rows * half
    in_row = lax.axis_index("col") * CORES + lax.axis_index("core")
    row_index = lax.axis_index("row")
    shard_index = row_index * half + in_row
    seq_place = (shard_index + half) % seq_span
    product = (inner_gate.astype(jnp.float32) * stream.astype(jnp.float32)).astype(jnp.bfloat16)
    blocks = product.reshape(row_count // kernel, kernel, groups, group_size)
    near_taps = toeplitz_taps(filters, 0)
    far_taps = toeplitz_taps(filters, kernel)
    tail_rows = product[row_count - kernel + 1 :]
    earlier = passed_along(tail_rows, CTX_AXES, ctx_size, 1)
    earlier = jnp.where(seq_place == 0, jnp.zeros_like(earlier), earlier)
    first_block = jnp.concatenate([jnp.zeros((1, channels), jnp.bfloat16), earlier], 0)
    first_block = first_block.reshape(1, kernel, groups, group_size)
    before = jnp.concatenate([first_block, blocks[:-1]], 0)
    filtered = (apply_blocks(near_taps, blocks) + apply_blocks(far_taps, before)).reshape(
        row_count, channels
    )
    mixed = (outer_gate.astype(jnp.float32) * filtered).astype(jnp.bfloat16)
    local_heads = channels // HEAD_DIM
    queries = query_rows.reshape(row_count, local_heads, HEAD_DIM)
    score_scale = 1.0 / math.sqrt(HEAD_DIM)
    query_pos = shard_index * row_count + jnp.arange(row_count, dtype=jnp.int32)
    seq_start = jnp.maximum(shard_index - seq_place, 0) * row_count

    def row_down(array):
        return lax.ppermute(array, "row", [(r, r + 1) for r in range(rows - 1)])

    def row_gather(array):
        pair = jnp.stack([array, row_down(array)])
        mine = lax.all_gather(pair, "col", axis=0)
        other = lax.ppermute(mine, "core", [(c, (c + 1) % CORES) for c in range(CORES)])
        return mine, other

    keys_mine, keys_other = row_gather(key_rows)
    values_mine, values_other = row_gather(mixed)
    core_index = lax.axis_index("core")
    halves = []
    for keys, values, core_of in (
        (keys_mine, values_mine, core_index),
        (keys_other, values_other, (core_index + 1) % CORES),
    ):
        gathered_rows = keys.shape[0] * keys.shape[1] * row_count
        key_index = jnp.arange(gathered_rows, dtype=jnp.int32)
        key_col = key_index // (2 * row_count)
        key_source = (key_index // row_count) % 2
        key_shard = key_col * CORES + core_of
        key_pos = ((row_index - key_source) * half + key_shard) * row_count + key_index % row_count
        visible = (key_pos[None, :] >= seq_start) & (key_pos[None, :] <= query_pos[:, None])
        halves.append(
            (visible, keys.reshape(gathered_rows, channels), values.reshape(gathered_rows, channels))
        )

    head_outputs = []
    for head in range(local_heads):
        lanes = slice(head * HEAD_DIM, (head + 1) * HEAD_DIM)
        scored = []
        for visible, keys, values in halves:
            scores = (
                lax.dot_general(
                    query_rows[:, lanes],
                    keys[:, lanes],
                    (((1,), (1,)), ((), ())),
                    preferred_element_type=jnp.float32,
                )
                * score_scale
            )
            scored.append(jnp.where(visible, scores, NEGATIVE))
        row_peak = jnp.maximum(
            jnp.max(scored[0], axis=1, keepdims=True), jnp.max(scored[1], axis=1, keepdims=True)
        )
        row_total = jnp.zeros((row_count, 1), jnp.float32)
        weighted = jnp.zeros((row_count, HEAD_DIM), jnp.float32)
        for scores, (visible, keys, values) in zip(scored, halves):
            exp_terms = jnp.where(visible, jnp.exp(scores - row_peak), 0.0)
            row_total = row_total + jnp.sum(exp_terms, axis=1, keepdims=True)
            weighted = weighted + jnp.dot(
                exp_terms.astype(jnp.bfloat16), values[:, lanes], preferred_element_type=jnp.float32
            )
        head_outputs.append((weighted / row_total).astype(jnp.bfloat16))
    attended = jnp.concatenate(head_outputs, axis=1)
    return (mixed, attended)


def solution(mesh):
    def run(outer_gate, inner_gate, stream, filters, query_rows, key_rows):
        ctx = mesh.shape["ctx"]
        row_count = outer_gate.shape[0] // ctx
        half = (LENGTH // 2) // row_count
        rows = ctx // half
        devices = mesh.devices.reshape(rows, half // CORES, CORES, mesh.shape["tp"])
        split = Mesh(devices, CTX_AXES + ("tp",))
        rows_spec = P(CTX_AXES, "tp")
        in_specs = (rows_spec, rows_spec, rows_spec, P("tp", None), rows_spec, rows_spec)
        outs = jax.shard_map(
            functools.partial(body, rows=rows, half=half),
            mesh=split,
            in_specs=in_specs,
            out_specs=(rows_spec, rows_spec),
            check_vma=False,
        )(outer_gate, inner_gate, stream, filters, query_rows, key_rows)
        placed = NamedSharding(mesh, P("ctx", "tp"))
        return tuple(lax.with_sharding_constraint(o, placed) for o in outs)

    return run
```

profile of v0, /device:TPU:1, one launch (start us, length us, event | category | flops | bytes accessed | tf_op | source)
XLA Modules:
  0.0 190.5 jit_solution(8433040790349666384)
XLA Ops:
  7.2 4.0 %collective-permute-start.1 = (bf16[256,512]{1,0:T(8,128)(2,1)}, bf16[256,512]{1,0:T(8,128)(2,1)S(1)}, u32[]{:S(2)}, u32[]{:S(2)}) collective-permute-start(bf16[256,512]{1,0:T(8,128)(2,1)} %param.11), channel_id=1, source_target_pairs={{0,64},{64,128},{128,192},{192,256},{256,320},{320,384},{384,448},... | collective-permute-start | bytes 786440 | tf_op jit(solution)/shard_map/ppermute | solution.py:69
  11.3 3.6 %collective-permute-done.1 = bf16[256,512]{1,0:T(8,128)(2,1)S(1)} collective-permute-done((bf16[256,512]{1,0:T(8,128)(2,1)}, bf16[256,512]{1,0:T(8,128)(2,1)S(1)}, u32[]{:S(2)}, u32[]{:S(2)}) %collective-permute-start.1) | collective-permute-done | bytes 262176 | tf_op jit(solution)/shard_map/ppermute | solution.py:69
  14.9 1.8 pad_maximum_fusion
  17.9 7.1 %collective-permute-start = (bf16[127,512]{1,0:T(8,128)(2,1)S(1)}, bf16[127,512]{1,0:T(8,128)(2,1)S(1)}, u32[]{:S(2)}, u32[]{:S(2)}) collective-permute-start(bf16[127,512]{1,0:T(8,128)(2,1)S(1)} %slice.114), channel_id=1, source_target_pairs={{0,4},{4,8},{8,12},{12,16},{16,20},{20,24},{24,28},{28,32},{32,36}... | collective-permute-start | bytes 390152 | tf_op jit(solution)/shard_map/ppermute | solution.py:21
  26.2 1.2 copy.42
  27.5 7.8 %reshape.153 = bf16[32,128,255]{2,1,0:T(8,128)(2,1)} reshape(bf16[32,32640]{1,0:T(8,128)(2,1)S(1)} %slice.112) | data formatting | bytes 4177920 | tf_op jit(solution)/shard_map/reshape | solution.py:31
  35.3 2.3 %fusion.117 = f32[32,2,16,128]{3,2,1,0:T(8,128)S(1)} fusion(bf16[32,128,255]{2,1,0:T(8,128)(2,1)} %reshape.153, bf16[2,128,32,16]{1,0,3,2:T(2,128)(2,1)S(1)} %reshape.152), kind=kOutput, calls=%fused_computation.106 | convolution fusion | flops 33554432 | bytes 1835008 | tf_op jit(solution)/shard_map/gts,bsgc->btgc/dot_general | solution.py:35
  39.3 7.8 %reshape.155 = bf16[32,128,255]{2,1,0:T(8,128)(2,1)} reshape(bf16[32,32640]{1,0:T(8,128)(2,1)S(1)} %slice.116) | data formatting | bytes 4177920 | tf_op jit(solution)/shard_map/reshape | solution.py:31
  47.5 2.3 %fusion.64 = f32[2,128,32,16]{1,3,0,2:T(8,128)S(1)} fusion(f32[32,2,16,128]{3,2,1,0:T(8,128)S(1)} %fusion.117, bf16[32,128,255]{2,1,0:T(8,128)(2,1)} %reshape.155, bf16[1,128,32,16]{1,3,0,2:T(8,128)(2,1)S(1)} %bitcast.76, bf16[1,128,32,16]{1,3,0,2:T(8,128)(2,1)S(1)} %bitcast.77), kind=kOutput, calls=%fused_computation.75 | convolution fusion | flops 33816576 | bytes 2359296 | tf_op jit(solution)/shard_map/gts,bsgc->btgc/dot_general | solution.py:35
  50.3 4.0 %collective-permute-start.3 = (bf16[256,512]{0,1:T(8,128)(2,1)S(1)}, bf16[256,512]{0,1:T(8,128)(2,1)S(1)}, u32[]{:S(2)}, u32[]{:S(2)}) collective-permute-start(bf16[256,512]{0,1:T(8,128)(2,1)S(1)} %fusion.118), channel_id=1, source_target_pairs={{0,64},{64,128},{128,192},{192,256},{256,320},{320,384},{384,448},... | collective-permute-start | bytes 786440 | tf_op jit(solution)/shard_map/ppermute | solution.py:69
  54.2 6.1 %collective-permute-done.3 = bf16[256,512]{0,1:T(8,128)(2,1)S(1)} collective-permute-done((bf16[256,512]{0,1:T(8,128)(2,1)S(1)}, bf16[256,512]{0,1:T(8,128)(2,1)S(1)}, u32[]{:S(2)}, u32[]{:S(2)}) %collective-permute-start.3) | collective-permute-done | bytes 262176 | tf_op jit(solution)/shard_map/ppermute | solution.py:69
  61.4 22.9 %all-gather.5.cloned.1.call-done = bf16[16,256,512]{2,1,0:T(8,128)(2,1)} async-done(((bf16[2,256,512]{2,1,0:T(8,128)(2,1)}), bf16[16,256,512]{2,1,0:T(8,128)(2,1)}) %all-gather.5.cloned.1.call-update) | async-done | bytes 4194320 | tf_op jit(solution)/shard_map/all_gather | solution.py:73
  84.3 2.8 %collective-permute-start.2 = (bf16[8,2,256,512]{3,2,1,0:T(8,128)(2,1)}, bf16[8,2,256,512]{3,2,1,0:T(8,128)(2,1)}, u32[]{:S(2)}, u32[]{:S(2)}) collective-permute-start(bf16[8,2,256,512]{3,2,1,0:T(8,128)(2,1)} %bitcast.81), channel_id=1, source_target_pairs={{0,4},{4,0},{1,5},{5,1},{2,6},{6,2},{3,7},{7,3},{8,12},{12,8},{9,1... | collective-permute-start | bytes 12582920 | tf_op jit(solution)/shard_map/ppermute | solution.py:74
  88.1 5.2 %fusion.164 = (f32[256]{0:T(256)S(1)}, f32[256,4096]{0,1:T(8,128)}) fusion(bf16[256,512]{1,0:T(8,128)(2,1)S(1)} %copy-done.7, bf16[4096,512]{1,0:T(8,128)(2,1)} %bitcast.82, s32[256]{0:T(256)S(1)} %iota_add_fusion, s32[4096]{0:T(1024)S(1)} %fusion.146, pred[4096]{0:T(1024)(128)(4,1)S(1)} %broadcast_compare_fusion.1), kind=kOutput, calls=%fused_computation.172 | convolution fusion | flops 273678080 | bytes 5330944 | tf_op jit(solution)/shard_map/dot_general | solution.py:102
  93.3 3.3 %fusion.166 = (f32[256]{0:T(256)S(1)}, f32[256,4096]{0,1:T(8,128)}) fusion(bf16[256,512]{1,0:T(8,128)(2,1)S(1)} %copy-done.7, bf16[4096,512]{1,0:T(8,128)(2,1)S(1)} %bitcast.83, s32[256]{0:T(256)S(1)} %iota_add_fusion, s32[4096]{0:T(1024)S(1)} %fusion.146, pred[4096]{0:T(1024)(128)(4,1)S(1)} %broadcast_compare_fusion.1), kind=kOutput, calls=%fused_computation.174 | convolution fusion | flops 273678080 | bytes 5330944 | tf_op jit(solution)/shard_map/dot_general | solution.py:102
  96.6 3.3 %fusion.168 = (f32[256]{0:T(256)S(1)}, f32[256,4096]{0,1:T(8,128)}) fusion(bf16[256,512]{1,0:T(8,128)(2,1)S(1)} %copy-done.7, bf16[4096,512]{1,0:T(8,128)(2,1)S(1)} %bitcast.84, s32[256]{0:T(256)S(1)} %iota_add_fusion, s32[4096]{0:T(1024)S(1)} %fusion.146, pred[4096]{0:T(1024)(128)(4,1)S(1)} %broadcast_compare_fusion.1), kind=kOutput, calls=%fused_computation.176 | convolution fusion | flops 273678080 | bytes 5330944 | tf_op jit(solution)/shard_map/dot_general | solution.py:102
  99.9 3.3 %fusion.162 = (f32[256]{0:T(256)S(1)}, f32[256,4096]{0,1:T(8,128)}) fusion(bf16[256,512]{1,0:T(8,128)(2,1)S(1)} %copy-done.7, bf16[4096,512]{1,0:T(8,128)(2,1)S(1)} %bitcast.85, s32[256]{0:T(256)S(1)} %iota_add_fusion, s32[4096]{0:T(1024)S(1)} %fusion.146, pred[4096]{0:T(1024)(128)(4,1)S(1)} %broadcast_compare_fusion.1), kind=kOutput, calls=%fused_computation.170 | convolution fusion | flops 273678080 | bytes 5330944 | tf_op jit(solution)/shard_map/dot_general | solution.py:102
  103.2 39.5 %all-gather.7.cloned.1.call-done = bf16[16,256,512]{2,1,0:T(8,128)(2,1)} async-done(((bf16[2,256,512]{2,1,0:T(8,128)(2,1)}), bf16[16,256,512]{2,1,0:T(8,128)(2,1)}) %all-gather.7.cloned.1.call-update) | async-done | bytes 4194320 | tf_op jit(solution)/shard_map/all_gather | solution.py:73
  142.8 2.6 %collective-permute-start.4 = (bf16[8,2,256,512]{3,2,1,0:T(8,128)(2,1)}, bf16[8,2,256,512]{3,2,1,0:T(8,128)(2,1)S(1)}, u32[]{:S(2)}, u32[]{:S(2)}) collective-permute-start(bf16[8,2,256,512]{3,2,1,0:T(8,128)(2,1)} %bitcast.86), channel_id=1, source_target_pairs={{0,4},{4,0},{1,5},{5,1},{2,6},{6,2},{3,7},{7,3},{8,12},{12,8},{9,1... | collective-permute-start | bytes 12582920 | tf_op jit(solution)/shard_map/ppermute | solution.py:74
  145.4 3.2 %fusion.165 = (f32[256]{0:T(256)S(1)}, f32[256,4096]{0,1:T(8,128)S(1)}) fusion(bf16[256,512]{1,0:T(8,128)(2,1)S(1)} %copy-done.7, bf16[4096,512]{1,0:T(8,128)(2,1)} %bitcast.12, s32[256]{0:T(256)S(1)} %iota_add_fusion, s32[4096]{0:T(1024)S(1)} %fusion.149, pred[4096]{0:T(1024)(128)(4,1)S(1)} %broadcast_compare_fusion), kind=kOutput, calls=%fused_computation.173 | convolution fusion | flops 273678080 | bytes 5330944 | tf_op jit(solution)/shard_map/dot_general | solution.py:102
  148.6 3.2 %fusion.167 = (f32[256]{0:T(256)S(1)}, f32[256,4096]{0,1:T(8,128)S(1)}) fusion(bf16[256,512]{1,0:T(8,128)(2,1)S(1)} %copy-done.7, bf16[4096,512]{1,0:T(8,128)(2,1)} %bitcast.12, s32[256]{0:T(256)S(1)} %iota_add_fusion, s32[4096]{0:T(1024)S(1)} %fusion.149, pred[4096]{0:T(1024)(128)(4,1)S(1)} %broadcast_compare_fusion), kind=kOutput, calls=%fused_computation.175 | convolution fusion | flops 273678080 | bytes 5330944 | tf_op jit(solution)/shard_map/dot_general | solution.py:102
  151.8 3.4 %fusion.169 = (f32[256]{0:T(256)S(1)}, f32[256,4096]{0,1:T(8,128)S(1)}) fusion(bf16[256,512]{1,0:T(8,128)(2,1)S(1)} %copy-done.7, bf16[4096,512]{1,0:T(8,128)(2,1)} %bitcast.12, s32[256]{0:T(256)S(1)} %iota_add_fusion, s32[4096]{0:T(1024)S(1)} %fusion.149, pred[4096]{0:T(1024)(128)(4,1)S(1)} %broadcast_compare_fusion), kind=kOutput, calls=%fused_computation.177 | convolution fusion | flops 273678080 | bytes 5330944 | tf_op jit(solution)/shard_map/dot_general | solution.py:102
  155.2 4.1 %fusion.163 = (f32[256]{0:T(256)S(1)}, f32[256,4096]{0,1:T(8,128)S(1)}) fusion(bf16[256,512]{1,0:T(8,128)(2,1)S(1)} %copy-done.7, bf16[4096,512]{1,0:T(8,128)(2,1)} %bitcast.12, s32[256]{0:T(256)S(1)} %iota_add_fusion, s32[4096]{0:T(1024)S(1)} %fusion.149, pred[4096]{0:T(1024)(128)(4,1)S(1)} %broadcast_compare_fusion), kind=kOutput, calls=%fused_computation.171 | convolution fusion | flops 273678080 | bytes 5330944 | tf_op jit(solution)/shard_map/dot_general | solution.py:102
  160.2 8.7 %fusion.16 = (f32[256]{0:T(256)S(1)}, f32[256]{0:T(256)S(1)}, f32[256]{0:T(256)S(1)}, f32[256]{0:T(256)S(1)}, f32[256]{0:T(256)S(1)}, /*index=5*/f32[256]{0:T(256)S(1)}, f32[256]{0:T(256)S(1)}, f32[256]{0:T(256)S(1)}) fusion(f32[256,4096]{0,1:T(8,128)S(1)} %copy-done, f32[256]{0:T(256)S(1)} %max.36, s32[256]{0:T(256)S(1)} %iota_add_fusion, ...), kind=kLoop, calls=%fused_computation.34 | loop fusion | flops 29358080 | bytes 33608704 | tf_op jit(solution)/shard_map/reduce_sum | solution.py:118
  169.0 1.7 fusion.46
  170.8 1.7 fusion.42
  172.5 1.7 fusion.38
  174.1 1.7 fusion.34
  175.9 1.7 fusion.98
  177.6 1.7 fusion.92
  179.3 1.7 fusion.86
  181.0 1.7 fusion.80
  (60 shorter events, 8.6 us)
Async XLA Ops:
  7.2 77.2 %all-gather.5.cloned.1.call-start = ((), (), s32[]{:S(2)}) async-start(), calls=%async_computation | async-start | bytes 4718592 | tf_op jit(solution)/shard_map/all_gather | solution.py:73
  7.2 7.7 %collective-permute-start.1 = (bf16[256,512]{1,0:T(8,128)(2,1)}, bf16[256,512]{1,0:T(8,128)(2,1)S(1)}, u32[]{:S(2)}, u32[]{:S(2)}) collective-permute-start(bf16[256,512]{1,0:T(8,128)(2,1)} %param.11), channel_id=1, source_target_pairs={{0,64},{64,128},{128,192},{192,256},{256,320},{320,384},{384,448},... | collective-permute-start | bytes 786440 | tf_op jit(solution)/shard_map/ppermute | solution.py:69
  16.7 126.0 %all-gather.7.cloned.1.call-start = ((), (), s32[]{:S(2)}) async-start(), calls=%async_computation.1 | async-start | bytes 4718592 | tf_op jit(solution)/shard_map/all_gather | solution.py:73
  17.9 29.3 %collective-permute-start = (bf16[127,512]{1,0:T(8,128)(2,1)S(1)}, bf16[127,512]{1,0:T(8,128)(2,1)S(1)}, u32[]{:S(2)}, u32[]{:S(2)}) collective-permute-start(bf16[127,512]{1,0:T(8,128)(2,1)S(1)} %slice.114), channel_id=1, source_target_pairs={{0,4},{4,8},{8,12},{12,16},{16,20},{20,24},{24,28},{28,32},{32,36}... | collective-permute-start | bytes 390152 | tf_op jit(solution)/shard_map/ppermute | solution.py:21
  39.2 8.0 %copy-start.4 = (bf16[256,512]{1,0:T(8,128)(2,1)S(1)}, bf16[256,512]{1,0:T(8,128)(2,1)}, u32[]{:S(2)}) copy-start(bf16[256,512]{1,0:T(8,128)(2,1)} %param.6) | copy-start | bytes 786436
  47.3 40.8 %copy-start.7 = (bf16[256,512]{1,0:T(8,128)(2,1)S(1)}, bf16[256,512]{1,0:T(8,128)(2,1)}, u32[]{:S(2)}) copy-start(bf16[256,512]{1,0:T(8,128)(2,1)} %param.10) | copy-start | bytes 786436
  50.3 10.1 %collective-permute-start.3 = (bf16[256,512]{0,1:T(8,128)(2,1)S(1)}, bf16[256,512]{0,1:T(8,128)(2,1)S(1)}, u32[]{:S(2)}, u32[]{:S(2)}) collective-permute-start(bf16[256,512]{0,1:T(8,128)(2,1)S(1)} %fusion.118), channel_id=1, source_target_pairs={{0,64},{64,128},{128,192},{192,256},{256,320},{320,384},{384,448},... | collective-permute-start | bytes 786440 | tf_op jit(solution)/shard_map/ppermute | solution.py:69
  84.3 61.0 %collective-permute-start.2 = (bf16[8,2,256,512]{3,2,1,0:T(8,128)(2,1)}, bf16[8,2,256,512]{3,2,1,0:T(8,128)(2,1)}, u32[]{:S(2)}, u32[]{:S(2)}) collective-permute-start(bf16[8,2,256,512]{3,2,1,0:T(8,128)(2,1)} %bitcast.81), channel_id=1, source_target_pairs={{0,4},{4,0},{1,5},{5,1},{2,6},{6,2},{3,7},{7,3},{8,12},{12,8},{9,1... | collective-permute-start | bytes 12582920 | tf_op jit(solution)/shard_map/ppermute | solution.py:74
  88.1 5.2 %copy-start.5 = (bf16[16,256,512]{2,1,0:T(8,128)(2,1)S(1)}, bf16[16,256,512]{2,1,0:T(8,128)(2,1)}, u32[]{:S(2)}) copy-start(bf16[16,256,512]{2,1,0:T(8,128)(2,1)} %all-gather.5.cloned.1.call-done) | copy-start | bytes 12582916
  142.8 33.1 %collective-permute-start.4 = (bf16[8,2,256,512]{3,2,1,0:T(8,128)(2,1)}, bf16[8,2,256,512]{3,2,1,0:T(8,128)(2,1)S(1)}, u32[]{:S(2)}, u32[]{:S(2)}) collective-permute-start(bf16[8,2,256,512]{3,2,1,0:T(8,128)(2,1)} %bitcast.86), channel_id=1, source_target_pairs={{0,4},{4,0},{1,5},{5,1},{2,6},{6,2},{3,7},{7,3},{8,12},{12,8},{9,1... | collective-permute-start | bytes 12582920 | tf_op jit(solution)/shard_map/ppermute | solution.py:74
  151.8 7.6 %copy-start.3 = (f32[256,4096]{0,1:T(8,128)S(1)}, f32[256,4096]{0,1:T(8,128)}, u32[]{:S(2)}) copy-start(f32[256,4096]{0,1:T(8,128)} %get-tuple-element.37) | copy-start | bytes 12582916
  155.2 4.2 %copy-start = (f32[256,4096]{0,1:T(8,128)S(1)}, f32[256,4096]{0,1:T(8,128)}, u32[]{:S(2)}) copy-start(f32[256,4096]{0,1:T(8,128)} %get-tuple-element.29) | copy-start | bytes 12582916
  155.2 4.2 %copy-start.1 = (f32[256,4096]{0,1:T(8,128)S(1)}, f32[256,4096]{0,1:T(8,128)}, u32[]{:S(2)}) copy-start(f32[256,4096]{0,1:T(8,128)} %get-tuple-element.33) | copy-start | bytes 12582916
  155.2 5.0 %copy-start.2 = (f32[256,4096]{0,1:T(8,128)S(1)}, f32[256,4096]{0,1:T(8,128)}, u32[]{:S(2)}) copy-start(f32[256,4096]{0,1:T(8,128)} %get-tuple-element.25) | copy-start | bytes 12582916
  160.2 8.8 %copy-start.6 = (bf16[16,256,512]{2,1,0:T(8,128)(2,1)S(1)}, bf16[16,256,512]{2,1,0:T(8,128)(2,1)}, u32[]{:S(2)}) copy-start(bf16[16,256,512]{2,1,0:T(8,128)(2,1)} %all-gather.7.cloned.1.call-done) | copy-start | bytes 12582916
Sparse Core Ops, SparseCore 0:
  16.9 67.4 all-gather.4
  86.4 56.3 all-gather.6
where the time goes:
time: 191 us; the launch traced here: 190 us
  waiting for transfers between devices  72.2 us (38%)
  matrix products  47.4 us (25%)
  local copies, waits for them, and re-layouts  23.9 us (13%)
  starting transfers between devices  20.5 us (11%)
  between operations  14.5 us (8%)
  other arithmetic  11.9 us (6%)
    all_gather x2, waiting for transfers between devices, row_gather(): mine = lax.all_gather(pair, 'col', axis=0)  62.4 us
    dot_general x8, matrix products, body(): lax.dot_general(query_rows[:, lanes], keys[:, lanes], (((1,), (1,)), ((),...  29.1 us
    reshape x2, local copies, waits for them, and re-layouts, toeplitz_taps(): flat.reshape(groups, kernel, 2 * kernel - 1)  15.6 us
    dot_general x8, matrix products, body(): jnp.dot(exp_terms.astype(jnp.bfloat16), values[:, lanes], preferred_eleme...  13.6 us
    ppermute x2, waiting for transfers between devices, row_down(): return lax.ppermute(array, 'row', [(r, r + 1) for r in range(rows - 1)])  9.68 us
    reduce_sum x1, other arithmetic, body(): row_total = row_total + jnp.sum(exp_terms, axis=1, keepdims=True)  8.74 us
    ppermute x2, starting transfers between devices, row_down(): return lax.ppermute(array, 'row', [(r, r + 1) for r in range(rows - 1)])  8.03 us
    ppermute x1, starting transfers between devices, passed_along(): return lax.ppermute(block, axis, route)  7.09 us
  transfers between devices with their start and end apart: 7, of which 4 were waited for; matrix products, arithmetic and copies ran while one was open for 38% of the time, Pallas kernels for 0%

commit v1 on v0

--- a/solution.py
+++ b/solution.py
@@ -45,10 +45,42 @@
     row_index = lax.axis_index("row")
     shard_index = row_index * half + in_row
     seq_place = (shard_index + half) % seq_span
+    cols = half // CORES
+    ahead = [(i, (i + 1) % cols) for i in range(cols)]
+    behind = [(i, (i - 1) % cols) for i in range(cols)]
+    swap = [(c, (c + 1) % CORES) for c in range(CORES)]
+
+    def row_down(array):
+        return lax.ppermute(array, "row", [(r, r + 1) for r in range(rows - 1)])
+
+    def row_gather(array, tied=()):
+        tied = list(tied)
+        pair = jnp.stack([array, row_down(array)])
+        pieces = [pair]
+        forward = backward = pair
+        for step in range(1, cols // 2):
+            forward = lax.ppermute(forward, "col", ahead)
+            backward = lax.ppermute(backward, "col", behind)
+            if tied:
+                item = tied.pop(0)
+                item = item() if callable(item) else item
+                forward, backward, released = lax.optimization_barrier((forward, backward, item))
+                released_stages.append(released)
+            pieces += [forward, backward]
+        last_own = lax.ppermute(forward[0], "col", ahead)
+        last_above = lax.ppermute(backward[1], "col", behind)
+        pieces.append(jnp.stack([last_own, last_above]))
+        mine = jnp.stack(pieces)
+        return mine, lax.ppermute(mine, "core", swap)
+
+    released_stages = []
+    keys_mine, keys_other = row_gather(key_rows, tied=[filters, filters, outer_gate])
+    filters_near, filters_far, outer_gate = released_stages
+
     product = (inner_gate.astype(jnp.float32) * stream.astype(jnp.float32)).astype(jnp.bfloat16)
     blocks = product.reshape(row_count // kernel, kernel, groups, group_size)
-    near_taps = toeplitz_taps(filters, 0)
-    far_taps = toeplitz_taps(filters, kernel)
+    near_taps = toeplitz_taps(filters_near, 0)
+    far_taps = toeplitz_taps(filters_far, kernel)
     tail_rows = product[row_count - kernel + 1 :]
     earlier = passed_along(tail_rows, CTX_AXES, ctx_size, 1)
     earlier = jnp.where(seq_place == 0, jnp.zeros_like(earlier), earlier)
@@ -65,42 +97,32 @@
     query_pos = shard_index * row_count + jnp.arange(row_count, dtype=jnp.int32)
     seq_start = jnp.maximum(shard_index - seq_place, 0) * row_count
 
-    def row_down(array):
-        return lax.ppermute(array, "row", [(r, r + 1) for r in range(rows - 1)])
-
-    def row_gather(array):
-        pair = jnp.stack([array, row_down(array)])
-        mine = lax.all_gather(pair, "col", axis=0)
-        other = lax.ppermute(mine, "core", [(c, (c + 1) % CORES) for c in range(CORES)])
-        return mine, other
-
-    keys_mine, keys_other = row_gather(key_rows)
-    values_mine, values_other = row_gather(mixed)
     core_index = lax.axis_index("core")
-    halves = []
-    for keys, values, core_of in (
-        (keys_mine, values_mine, core_index),
-        (keys_other, values_other, (core_index + 1) % CORES),
-    ):
-        gathered_rows = keys.shape[0] * keys.shape[1] * row_count
+    col_index = lax.axis_index("col")
+
+    def key_visibility(core_of):
+        gathered_rows = cols * 2 * row_count
         key_index = jnp.arange(gathered_rows, dtype=jnp.int32)
-        key_col = key_index // (2 * row_count)
+        piece = key_index // (2 * row_count)
+        reach = (piece + 1) // 2
+        offset = jnp.where(piece % 2 == 1, -reach, reach)
+        key_col = (col_index + offset + cols) % cols
         key_source = (key_index // row_count) % 2
         key_shard = key_col * CORES + core_of
         key_pos = ((row_index - key_source) * half + key_shard) * row_count + key_index % row_count
-        visible = (key_pos[None, :] >= seq_start) & (key_pos[None, :] <= query_pos[:, None])
-        halves.append(
-            (visible, keys.reshape(gathered_rows, channels), values.reshape(gathered_rows, channels))
-        )
-
-    head_outputs = []
-    for head in range(local_heads):
+        return (key_pos[None, :] >= seq_start) & (key_pos[None, :] <= query_pos[:, None])
+
+    half_keys = (
+        (key_visibility(core_index), keys_mine.reshape(-1, channels)),
+        (key_visibility((core_index + 1) % CORES), keys_other.reshape(-1, channels)),
+    )
+    def head_softmax(head, head_queries):
         lanes = slice(head * HEAD_DIM, (head + 1) * HEAD_DIM)
         scored = []
-        for visible, keys, values in halves:
+        for visible, keys in half_keys:
             scores = (
                 lax.dot_general(
-                    query_rows[:, lanes],
+                    head_queries,
                     keys[:, lanes],
                     (((1,), (1,)), ((), ())),
                     preferred_element_type=jnp.float32,
@@ -112,14 +134,51 @@
             jnp.max(scored[0], axis=1, keepdims=True), jnp.max(scored[1], axis=1, keepdims=True)
         )
         row_total = jnp.zeros((row_count, 1), jnp.float32)
-        weighted = jnp.zeros((row_count, HEAD_DIM), jnp.float32)
-        for scores, (visible, keys, values) in zip(scored, halves):
+        weights = []
+        for scores, (visible, keys) in zip(scored, half_keys):
             exp_terms = jnp.where(visible, jnp.exp(scores - row_peak), 0.0)
             row_total = row_total + jnp.sum(exp_terms, axis=1, keepdims=True)
-            weighted = weighted + jnp.dot(
-                exp_terms.astype(jnp.bfloat16), values[:, lanes], preferred_element_type=jnp.float32
-            )
-        head_outputs.append((weighted / row_total).astype(jnp.bfloat16))
+            weights.append(exp_terms.astype(jnp.bfloat16))
+        return (tuple(weights), row_total)
+
+    def head_queries(head):
+        return query_rows[:, head * HEAD_DIM : (head + 1) * HEAD_DIM]
+
+    head_results = [head_softmax(0, head_queries(0))]
+
+    def take_released():
+        finished, queries_now = released_stages[-1]
+        head_results[len(head_results) - 1] = finished
+        head_results.append(head_softmax(len(head_results), queries_now))
+
+    def next_head(head):
+        def tie():
+            if head >= 2:
+                take_released()
+            return (head_results[head - 1], head_queries(head))
+
+        return tie
+
+    released_stages = []
+    ring_rounds = cols // 2 - 1
+    values_mine, values_other = row_gather(
+        mixed, tied=[next_head(head) for head in range(1, min(local_heads, ring_rounds + 1))]
+    )
+    if released_stages:
+        take_released()
+    for head in range(len(head_results), local_heads):
+        head_results.append(head_softmax(head, head_queries(head)))
+    head_weights = [weights for weights, total in head_results]
+    head_totals = [total for weights, total in head_results]
+    half_values = (values_mine.reshape(-1, channels), values_other.reshape(-1, channels))
+
+    head_outputs = []
+    for head in range(local_heads):
+        lanes = slice(head * HEAD_DIM, (head + 1) * HEAD_DIM)
+        weighted = jnp.zeros((row_count, HEAD_DIM), jnp.float32)
+        for weights, values in zip(head_weights[head], half_values):
+            weighted = weighted + jnp.dot(weights, values[:, lanes], preferred_element_type=jnp.float32)
+        head_outputs.append((weighted / head_totals[head]).astype(jnp.bfloat16))
     attended = jnp.concatenate(head_outputs, axis=1)
     return (mixed, attended)
 

time: 191 us -> 253 us (1.32)
  starting transfers between devices: 20.5 us -> 88.2 us
  waiting for transfers between devices: 72.2 us -> 42.6 us
  local copies, waits for them, and re-layouts: 23.9 us -> 46.4 us
  other arithmetic: 11.9 us -> 26.8 us
  between operations: 14.5 us -> 1.36 us
  matrix products: 47.4 us -> 44.8 us
    ppermute x2 -> x18, starting transfers between devices: 5.32 us -> 78.2 us  [the longest x6 32.7 us: row_gather(): backward = lax.ppermute(backward, 'col', behind)]
    all_gather x2 -> x0, waiting for transfers between devices: 62.4 us -> none  [row_gather(): mine = lax.all_gather(pair, 'col', axis=0)]
    ppermute x2 -> x18, waiting for transfers between devices: 0.01 us -> 30.8 us  [the longest x6 18.3 us: row_gather(): forward = lax.ppermute(forward, 'col', ahead)]
    reduce_sum x1 -> x4, other arithmetic: 8.74 us -> 21 us  [head_softmax(): row_total = row_total + jnp.sum(exp_terms, axis=1, keepdims=True)]
    unnamed x22 -> x43, local copies, waits for them, and re-layouts: 5.2 us -> 16.1 us
    ppermute x0 -> x1, local copies, waits for them, and re-layouts: none -> 6.49 us  [row_gather(): return (mine, lax.ppermute(mine, 'core', swap))]
    another operation x1, local copies, waits for them, and re-layouts: 1.04 us -> 6.48 us  [row_gather(): mine = jnp.stack(pieces)]
    ppermute x1, starting transfers between devices: 7.09 us -> 1.92 us  [passed_along(): return lax.ppermute(block, axis, route)]
  transfers between devices with their start and end apart: 7 -> 21, of which waited for: 4 -> 13; matrix products, arithmetic and copies ran while one was open for 38% -> 34% of each run, Pallas kernels for 0% -> 0%
where the time goes in v1:
time: 253 us; the launch traced here: 250 us
  starting transfers between devices  88.2 us (35%)
  local copies, waits for them, and re-layouts  46.4 us (18%)
  matrix products  44.8 us (18%)
  waiting for transfers between devices  42.6 us (17%)
  other arithmetic  26.8 us (11%)
    ppermute x6, starting transfers between devices, row_gather(): backward = lax.ppermute(backward, 'col', behind)  32.7 us
    dot_general x8, matrix products, head_softmax(): lax.dot_general(head_queries, keys[:, lanes], (((1,), (1,)), ((), ())), p...  26 us
    reduce_sum x4, other arithmetic, head_softmax(): row_total = row_total + jnp.sum(exp_terms, axis=1, keepdims=True)  21 us
    ppermute x6, waiting for transfers between devices, row_gather(): forward = lax.ppermute(forward, 'col', ahead)  18.3 us
    ppermute x2, starting transfers between devices, row_gather(): return (mine, lax.ppermute(mine, 'core', swap))  16.3 us
    unnamed x43, local copies, waits for them, and re-layouts  16.1 us
    ppermute x6, starting transfers between devices, row_gather(): forward = lax.ppermute(forward, 'col', ahead)  16 us
    reshape x2, local copies, waits for them, and re-layouts, toeplitz_taps(): flat.reshape(groups, kernel, 2 * kernel - 1)  15.5 us
  transfers between devices with their start and end apart: 21, of which 13 were waited for; matrix products, arithmetic and copies ran while one was open for 34% of the time, Pallas kernels for 0%

profile of v1, /device:TPU:1, one launch (start us, length us, event | category | flops | bytes accessed | tf_op | source)
XLA Modules:
  0.0 250.2 jit_solution(12914236197215596988)
XLA Ops:
  0.6 4.0 %collective-permute-start = (bf16[256,512]{1,0:T(8,128)(2,1)}, bf16[256,512]{1,0:T(8,128)(2,1)S(1)}, u32[]{:S(2)}, u32[]{:S(2)}) collective-permute-start(bf16[256,512]{1,0:T(8,128)(2,1)} %param.11), channel_id=1, source_target_pairs={{0,64},{64,128},{128,192},{192,256},{256,320},{320,384},{384,448},... | collective-permute-start | bytes 786440 | tf_op jit(solution)/shard_map/ppermute | solution.py:54
  4.7 3.8 %collective-permute-done = bf16[256,512]{1,0:T(8,128)(2,1)S(1)} collective-permute-done((bf16[256,512]{1,0:T(8,128)(2,1)}, bf16[256,512]{1,0:T(8,128)(2,1)S(1)}, u32[]{:S(2)}, u32[]{:S(2)}) %collective-permute-start) | collective-permute-done | bytes 262176 | tf_op jit(solution)/shard_map/ppermute | solution.py:54
  9.5 5.5 %collective-permute-start.1 = (bf16[2,256,512]{2,1,0:T(8,128)(2,1)S(1)}, bf16[2,256,512]{2,1,0:T(8,128)(2,1)S(1)}, u32[]{:S(2)}, u32[]{:S(2)}) collective-permute-start(bf16[2,256,512]{2,1,0:T(8,128)(2,1)S(1)} %pad_maximum_fusion), channel_id=1, source_target_pairs={{0,8},{8,16},{16,24},{24,32},{32,40},{40,48},{48,56},{56,0},{1,9},... | collective-permute-start | bytes 1572872 | tf_op jit(solution)/shard_map/ppermute | solution.py:62
  15.0 8.6 %collective-permute-start.2 = (bf16[2,256,512]{2,1,0:T(8,128)(2,1)S(1)}, bf16[2,256,512]{2,1,0:T(8,128)(2,1)S(1)}, u32[]{:S(2)}, u32[]{:S(2)}) collective-permute-start(bf16[2,256,512]{2,1,0:T(8,128)(2,1)S(1)} %pad_maximum_fusion), channel_id=1, source_target_pairs={{0,56},{8,0},{16,8},{24,16},{32,24},{40,32},{48,40},{56,48},{1,57}... | collective-permute-start | bytes 1572872 | tf_op jit(solution)/shard_map/ppermute | solution.py:63
  23.5 8.7 %collective-permute-done.1 = bf16[2,256,512]{2,1,0:T(8,128)(2,1)S(1)} collective-permute-done((bf16[2,256,512]{2,1,0:T(8,128)(2,1)S(1)}, bf16[2,256,512]{2,1,0:T(8,128)(2,1)S(1)}, u32[]{:S(2)}, u32[]{:S(2)}) %collective-permute-start.1) | collective-permute-done | bytes 524320 | tf_op jit(solution)/shard_map/ppermute | solution.py:62
  35.1 5.3 %collective-permute-start.4 = (bf16[2,256,512]{2,1,0:T(8,128)(2,1)S(1)}, bf16[2,256,512]{2,1,0:T(8,128)(2,1)S(1)}, u32[]{:S(2)}, u32[]{:S(2)}) collective-permute-start(bf16[2,256,512]{2,1,0:T(8,128)(2,1)S(1)} %collective-permute-done.2), channel_id=1, source_target_pairs={{0,56},{8,0},{16,8},{24,16},{32,24},{40,32},{48,40},{56,48},{1,57}... | collective-permute-start | bytes 1572872 | tf_op jit(solution)/shard_map/ppermute | solution.py:63
  43.1 5.2 %collective-permute-done.3 = bf16[2,256,512]{2,1,0:T(8,128)(2,1)S(1)} collective-permute-done((bf16[2,256,512]{2,1,0:T(8,128)(2,1)S(1)}, bf16[2,256,512]{2,1,0:T(8,128)(2,1)S(1)}, u32[]{:S(2)}, u32[]{:S(2)}) %collective-permute-start.3) | collective-permute-done | bytes 524320 | tf_op jit(solution)/shard_map/ppermute | solution.py:62
  52.1 4.4 %collective-permute-start.6 = (bf16[2,256,512]{2,1,0:T(8,128)(2,1)S(1)}, bf16[2,256,512]{2,1,0:T(8,128)(2,1)S(1)}, u32[]{:S(2)}, u32[]{:S(2)}) collective-permute-start(bf16[2,256,512]{2,1,0:T(8,128)(2,1)S(1)} %collective-permute-done.4), channel_id=1, source_target_pairs={{0,56},{8,0},{16,8},{24,16},{32,24},{40,32},{48,40},{56,48},{1,57}... | collective-permute-start | bytes 1572872 | tf_op jit(solution)/shard_map/ppermute | solution.py:63
  58.9 4.4 %collective-permute-done.5 = bf16[2,256,512]{2,1,0:T(8,128)(2,1)S(1)} collective-permute-done((bf16[2,256,512]{2,1,0:T(8,128)(2,1)S(1)}, bf16[2,256,512]{2,1,0:T(8,128)(2,1)S(1)}, u32[]{:S(2)}, u32[]{:S(2)}) %collective-permute-start.5) | collective-permute-done | bytes 524320 | tf_op jit(solution)/shard_map/ppermute | solution.py:62
  64.2 5.3 %collective-permute-start.12 = (bf16[256,512]{1,0:T(8,128)(2,1)S(1)}, bf16[256,512]{1,0:T(8,128)(2,1)S(1)}, u32[]{:S(2)}, u32[]{:S(2)}) collective-permute-start(bf16[256,512]{1,0:T(8,128)(2,1)S(1)} %slice_bitcast_fusion.6), channel_id=1, source_target_pairs={{0,56},{8,0},{16,8},{24,16},{32,24},{40,32},{48,40},{56,48},{1,57}... | collective-permute-start | bytes 786440 | tf_op jit(solution)/shard_map/ppermute | solution.py:71
  73.2 4.7 %collective-permute-done.11 = bf16[256,512]{1,0:T(8,128)(2,1)S(1)} collective-permute-done((bf16[256,512]{1,0:T(8,128)(2,1)S(1)}, bf16[256,512]{1,0:T(8,128)(2,1)S(1)}, u32[]{:S(2)}, u32[]{:S(2)}) %collective-permute-start.11) | collective-permute-done | bytes 262176 | tf_op jit(solution)/shard_map/ppermute | solution.py:70
  78.8 7.6 %collective-permute-start.13 = (bf16[8,2,256,512]{3,2,1,0:T(8,128)(2,1)}, bf16[8,2,256,512]{3,2,1,0:T(8,128)(2,1)}, u32[]{:S(2)}, u32[]{:S(2)}) collective-permute-start(bf16[8,2,256,512]{3,2,1,0:T(8,128)(2,1)} %fusion.71), channel_id=1, source_target_pairs={{0,4},{4,0},{1,5},{5,1},{2,6},{6,2},{3,7},{7,3},{8,12},{12,8},{9,1... | collective-permute-start | bytes 12582920 | tf_op jit(solution)/shard_map/ppermute | solution.py:74
  89.0 4.2 %collective-permute-done.7 = bf16[127,512]{1,0:T(8,128)(2,1)S(1)} collective-permute-done((bf16[127,512]{1,0:T(8,128)(2,1)S(1)}, bf16[127,512]{1,0:T(8,128)(2,1)S(1)}, u32[]{:S(2)}, u32[]{:S(2)}) %collective-permute-start.7) | collective-permute-done | bytes 130080 | tf_op jit(solution)/shard_map/ppermute | solution.py:21
  95.1 7.8 %reshape.217 = bf16[32,128,255]{2,1,0:T(8,128)(2,1)} reshape(bf16[32,32640]{1,0:T(8,128)(2,1)S(1)} %slice.124) | data formatting | bytes 4177920 | tf_op jit(solution)/shard_map/reshape | solution.py:31
  106.8 7.8 %reshape.219 = bf16[32,128,255]{2,1,0:T(8,128)(2,1)} reshape(bf16[32,32640]{1,0:T(8,128)(2,1)S(1)} %slice.128) | data formatting | bytes 4177920 | tf_op jit(solution)/shard_map/reshape | solution.py:31
  117.4 4.0 %collective-permute-start.8 = (bf16[256,512]{0,1:T(8,128)(2,1)S(1)}, bf16[256,512]{0,1:T(8,128)(2,1)S(1)}, u32[]{:S(2)}, u32[]{:S(2)}) collective-permute-start(bf16[256,512]{0,1:T(8,128)(2,1)S(1)} %fusion.70), channel_id=1, source_target_pairs={{0,64},{64,128},{128,192},{192,256},{256,320},{320,384},{384,448},... | collective-permute-start | bytes 786440 | tf_op jit(solution)/shard_map/ppermute | solution.py:54
  121.5 3.8 %collective-permute-done.8 = bf16[256,512]{0,1:T(8,128)(2,1)S(1)} collective-permute-done((bf16[256,512]{0,1:T(8,128)(2,1)S(1)}, bf16[256,512]{0,1:T(8,128)(2,1)S(1)}, u32[]{:S(2)}, u32[]{:S(2)}) %collective-permute-start.8) | collective-permute-done | bytes 262176 | tf_op jit(solution)/shard_map/ppermute | solution.py:54
  127.3 4.8 %collective-permute-start.10 = (bf16[2,256,512]{1,2,0:T(8,128)(2,1)S(1)}, bf16[2,256,512]{1,2,0:T(8,128)(2,1)S(1)}, u32[]{:S(2)}, u32[]{:S(2)}) collective-permute-start(bf16[2,256,512]{1,2,0:T(8,128)(2,1)S(1)} %pad_maximum_fusion.1), channel_id=1, source_target_pairs={{0,56},{8,0},{16,8},{24,16},{32,24},{40,32},{48,40},{56,48},{1,57}... | collective-permute-start | bytes 1572872 | tf_op jit(solution)/shard_map/ppermute | solution.py:63
  139.4 5.2 %fusion.12 = (f32[256]{0:T(256)S(1)}, f32[256]{0:T(256)S(1)}, bf16[256,4096]{0,1:T(8,128)(2,1)S(1)}, bf16[256,4096]{0,1:T(8,128)(2,1)}) fusion(f32[256,4096]{0,1:T(8,128)S(1)} %get-tuple-element.82, f32[256]{0:T(256)S(1)} %max.36, s32[256]{0:T(256)S(1)} %iota_add_fusion, s32[4096]{0:T(1024)S(1)} %fusion.100, pred[4096]{0:T(1024)(128)(4,1)S(1)} %broadcast_compare_fusion, ...), kind=kLoop, calls=%fused_computation.30 | loop fusion | flops 12582400 | bytes 12627968 | tf_op jit(solution)/shard_map/reduce_sum | solution.py:140
  144.5 3.2 %fusion.112 = (f32[256]{0:T(256)S(1)}, f32[256,4096]{0,1:T(8,128)S(1)}) fusion(bf16[256,128]{1,0:T(8,128)(2,1)S(1)} %get-tuple-element.41, bf16[4096,512]{1,0:T(8,128)(2,1)} %bitcast.25, s32[256]{0:T(256)S(1)} %iota_add_fusion, s32[4096]{0:T(1024)S(1)} %fusion.100, pred[4096]{0:T(1024)(128)(4,1)S(1)} %broadcast_compare_fusion), kind=kOutput, calls=%fused_computation.178 | convolution fusion | flops 273678080 | bytes 5330944 | tf_op jit(solution)/shard_map/dot_general | solution.py:124
  153.0 4.6 %collective-permute-start.15 = (bf16[2,256,512]{1,2,0:T(8,128)(2,1)S(1)}, bf16[2,256,512]{1,2,0:T(8,128)(2,1)S(1)}, u32[]{:S(2)}, u32[]{:S(2)}) collective-permute-start(bf16[2,256,512]{1,2,0:T(8,128)(2,1)S(1)} %collective-permute-done.10), channel_id=1, source_target_pairs={{0,56},{8,0},{16,8},{24,16},{32,24},{40,32},{48,40},{56,48},{1,57}... | collective-permute-start | bytes 1572872 | tf_op jit(solution)/shard_map/ppermute | solution.py:63
  157.5 6.2 %fusion.16 = (f32[256]{0:T(256)S(1)}, f32[256]{0:T(256)S(1)}, bf16[256,4096]{0,1:T(8,128)(2,1)}, bf16[256,4096]{0,1:T(8,128)(2,1)}) fusion(f32[256,4096]{0,1:T(8,128)S(1)} %get-tuple-element.86, f32[256]{0:T(256)S(1)} %max.37, s32[256]{0:T(256)S(1)} %iota_add_fusion, s32[4096]{0:T(1024)S(1)} %fusion.100, pred[4096]{0:T(1024)(128)(4,1)S(1)} %broadcast_compare_fusion, ...), kind=kLoop, calls=%fused_computation.34 | loop fusion | flops 12582400 | bytes 12627968 | tf_op jit(solution)/shard_map/reduce_sum | solution.py:140
  173.8 5.1 %collective-permute-start.17 = (bf16[2,256,512]{1,2,0:T(8,128)(2,1)S(1)}, bf16[2,256,512]{1,2,0:T(8,128)(2,1)S(1)}, u32[]{:S(2)}, u32[]{:S(2)}) collective-permute-start(bf16[2,256,512]{1,2,0:T(8,128)(2,1)S(1)} %collective-permute-done.15), channel_id=1, source_target_pairs={{0,56},{8,0},{16,8},{24,16},{32,24},{40,32},{48,40},{56,48},{1,57}... | collective-permute-start | bytes 1572872 | tf_op jit(solution)/shard_map/ppermute | solution.py:63
  179.0 6.0 %fusion.20 = (f32[256]{0:T(256)S(1)}, f32[256]{0:T(256)S(1)}, bf16[256,4096]{0,1:T(8,128)(2,1)}, bf16[256,4096]{0,1:T(8,128)(2,1)}) fusion(f32[256,4096]{0,1:T(8,128)S(1)} %get-tuple-element.90, f32[256]{0:T(256)S(1)} %max.38, s32[256]{0:T(256)S(1)} %iota_add_fusion, s32[4096]{0:T(1024)S(1)} %fusion.100, pred[4096]{0:T(1024)(128)(4,1)S(1)} %broadcast_compare_fusion, ...), kind=kLoop, calls=%fused_computation.38 | loop fusion | flops 12582400 | bytes 12627968 | tf_op jit(solution)/shard_map/reduce_sum | solution.py:140
  187.2 3.9 %collective-permute-start.19 = (bf16[256,512]{0,1:T(8,128)(2,1)S(1)}, bf16[256,512]{0,1:T(8,128)(2,1)S(1)}, u32[]{:S(2)}, u32[]{:S(2)}) collective-permute-start(bf16[256,512]{0,1:T(8,128)(2,1)S(1)} %slice_bitcast_fusion.4), channel_id=1, source_target_pairs={{0,56},{8,0},{16,8},{24,16},{32,24},{40,32},{48,40},{56,48},{1,57}... | collective-permute-start | bytes 786440 | tf_op jit(solution)/shard_map/ppermute | solution.py:71
  195.0 4.5 %collective-permute-done.18 = bf16[256,512]{0,1:T(8,128)(2,1)S(1)} collective-permute-done((bf16[256,512]{0,1:T(8,128)(2,1)S(1)}, bf16[256,512]{0,1:T(8,128)(2,1)S(1)}, u32[]{:S(2)}, u32[]{:S(2)}) %collective-permute-start.18) | collective-permute-done | bytes 262176 | tf_op jit(solution)/shard_map/ppermute | solution.py:70
  200.3 8.7 %collective-permute-start.20 = (bf16[8,2,256,512]{2,3,1,0:T(8,128)(2,1)}, bf16[8,2,256,512]{2,3,1,0:T(8,128)(2,1)}, u32[]{:S(2)}, u32[]{:S(2)}) collective-permute-start(bf16[8,2,256,512]{2,3,1,0:T(8,128)(2,1)} %fusion.72), channel_id=1, source_target_pairs={{0,4},{4,0},{1,5},{5,1},{2,6},{6,2},{3,7},{7,3},{8,12},{12,8},{9,1... | collective-permute-start | bytes 12582920 | tf_op jit(solution)/shard_map/ppermute | solution.py:74
  213.0 3.5 %fusion.116 = (f32[256]{0:T(256)S(1)}, f32[256,4096]{0,1:T(8,128)S(1)}) fusion(bf16[256,128]{1,0:T(8,128)(2,1)S(1)} %get-tuple-element.55, bf16[4096,512]{1,0:T(8,128)(2,1)} %bitcast.25, s32[256]{0:T(256)S(1)} %iota_add_fusion, s32[4096]{0:T(1024)S(1)} %fusion.100, pred[4096]{0:T(1024)(128)(4,1)S(1)} %broadcast_compare_fusion), kind=kOutput, calls=%fused_computation.182 | convolution fusion | flops 273678080 | bytes 5330944 | tf_op jit(solution)/shard_map/dot_general | solution.py:124
  216.5 3.7 %fusion.24 = (f32[256]{0:T(256)S(1)}, f32[256]{0:T(256)S(1)}) fusion(f32[256,4096]{0,1:T(8,128)S(1)} %get-tuple-element.94, f32[256]{0:T(256)S(1)} %max.39, s32[256]{0:T(256)S(1)} %iota_add_fusion, s32[4096]{0:T(1024)S(1)} %fusion.100, pred[4096]{0:T(1024)(128)(4,1)S(1)} %broadcast_compare_fusion, f32[256,4096]{0,1:T(8,128)S(1)} %get-tuple-element.92, ...), kind=kLoop, calls=%fused_computation.42 | loop fusion | flops 10485248 | bytes 8433664 | tf_op jit(solution)/shard_map/reduce_sum | solution.py:140
  220.3 6.5 %copy.42 = bf16[8,2,256,512]{3,2,1,0:T(8,128)(2,1)} copy(bf16[8,2,256,512]{2,3,1,0:T(8,128)(2,1)} %fusion.72) | data formatting | bytes 8388608 | tf_op jit(solution)/shard_map/stack | solution.py:73
  226.7 5.0 %fusion.28 = f32[256,128]{0,1:T(8,128)S(1)} fusion(f32[256,4096]{0,1:T(8,128)} %copy-done.3, f32[256]{0:T(256)S(1)} %max.39, s32[256]{0:T(256)S(1)} %iota_add_fusion, s32[4096]{0:T(1024)S(1)} %fusion.101, pred[4096]{0:T(1024)(128)(4,1)S(1)} %broadcast_compare_fusion.1, bf16[4096,512]{1,0:T(8,128)(2,1)} %bitcast.114), kind=kOutput, calls=%fused_computation.45 | convolution fusion | flops 273678336 | bytes 5396480 | tf_op jit(solution)/shard_map/dot_general | solution.py:180
  231.8 6.5 %copy.43 = bf16[8,2,256,512]{3,2,1,0:T(8,128)(2,1)} copy(bf16[8,2,256,512]{2,3,1,0:T(8,128)(2,1)} %collective-permute-done.20) | data formatting | bytes 8388608 | tf_op jit(solution)/shard_map/ppermute | solution.py:74
  (123 shorter events, 76.5 us)
Async XLA Ops:
  0.6 7.8 %collective-permute-start = (bf16[256,512]{1,0:T(8,128)(2,1)}, bf16[256,512]{1,0:T(8,128)(2,1)S(1)}, u32[]{:S(2)}, u32[]{:S(2)}) collective-permute-start(bf16[256,512]{1,0:T(8,128)(2,1)} %param.11), channel_id=1, source_target_pairs={{0,64},{64,128},{128,192},{192,256},{256,320},{320,384},{384,448},... | collective-permute-start | bytes 786440 | tf_op jit(solution)/shard_map/ppermute | solution.py:54
  9.5 22.8 %collective-permute-start.1 = (bf16[2,256,512]{2,1,0:T(8,128)(2,1)S(1)}, bf16[2,256,512]{2,1,0:T(8,128)(2,1)S(1)}, u32[]{:S(2)}, u32[]{:S(2)}) collective-permute-start(bf16[2,256,512]{2,1,0:T(8,128)(2,1)S(1)} %pad_maximum_fusion), channel_id=1, source_target_pairs={{0,8},{8,16},{16,24},{24,32},{32,40},{40,48},{48,56},{56,0},{1,9},... | collective-permute-start | bytes 1572872 | tf_op jit(solution)/shard_map/ppermute | solution.py:62
  15.0 18.2 %collective-permute-start.2 = (bf16[2,256,512]{2,1,0:T(8,128)(2,1)S(1)}, bf16[2,256,512]{2,1,0:T(8,128)(2,1)S(1)}, u32[]{:S(2)}, u32[]{:S(2)}) collective-permute-start(bf16[2,256,512]{2,1,0:T(8,128)(2,1)S(1)} %pad_maximum_fusion), channel_id=1, source_target_pairs={{0,56},{8,0},{16,8},{24,16},{32,24},{40,32},{48,40},{56,48},{1,57}... | collective-permute-start | bytes 1572872 | tf_op jit(solution)/shard_map/ppermute | solution.py:63
  33.2 15.1 %collective-permute-start.3 = (bf16[2,256,512]{2,1,0:T(8,128)(2,1)S(1)}, bf16[2,256,512]{2,1,0:T(8,128)(2,1)S(1)}, u32[]{:S(2)}, u32[]{:S(2)}) collective-permute-start(bf16[2,256,512]{2,1,0:T(8,128)(2,1)S(1)} %collective-permute-done.1), channel_id=1, source_target_pairs={{0,8},{8,16},{16,24},{24,32},{32,40},{40,48},{48,56},{56,0},{1,9},... | collective-permute-start | bytes 1572872 | tf_op jit(solution)/shard_map/ppermute | solution.py:62
  35.1 14.1 %collective-permute-start.4 = (bf16[2,256,512]{2,1,0:T(8,128)(2,1)S(1)}, bf16[2,256,512]{2,1,0:T(8,128)(2,1)S(1)}, u32[]{:S(2)}, u32[]{:S(2)}) collective-permute-start(bf16[2,256,512]{2,1,0:T(8,128)(2,1)S(1)} %collective-permute-done.2), channel_id=1, source_target_pairs={{0,56},{8,0},{16,8},{24,16},{32,24},{40,32},{48,40},{56,48},{1,57}... | collective-permute-start | bytes 1572872 | tf_op jit(solution)/shard_map/ppermute | solution.py:63
  42.2 44.2 %copy-start.8 = (bf16[256,512]{1,0:T(8,128)(2,1)S(1)}, bf16[256,512]{1,0:T(8,128)(2,1)}, u32[]{:S(2)}) copy-start(bf16[256,512]{1,0:T(8,128)(2,1)} %param.8) | copy-start | bytes 786436
  42.2 44.2 %copy-start.9 = (bf16[256,512]{1,0:T(8,128)(2,1)S(1)}, bf16[256,512]{1,0:T(8,128)(2,1)}, u32[]{:S(2)}) copy-start(bf16[256,512]{1,0:T(8,128)(2,1)} %param.7) | copy-start | bytes 786436
  49.2 14.1 %collective-permute-start.5 = (bf16[2,256,512]{2,1,0:T(8,128)(2,1)S(1)}, bf16[2,256,512]{2,1,0:T(8,128)(2,1)S(1)}, u32[]{:S(2)}, u32[]{:S(2)}) collective-permute-start(bf16[2,256,512]{2,1,0:T(8,128)(2,1)S(1)} %collective-permute-done.3), channel_id=1, source_target_pairs={{0,8},{8,16},{16,24},{24,32},{32,40},{40,48},{48,56},{56,0},{1,9},... | collective-permute-start | bytes 1572872 | tf_op jit(solution)/shard_map/ppermute | solution.py:62
  52.1 12.2 %collective-permute-start.6 = (bf16[2,256,512]{2,1,0:T(8,128)(2,1)S(1)}, bf16[2,256,512]{2,1,0:T(8,128)(2,1)S(1)}, u32[]{:S(2)}, u32[]{:S(2)}) collective-permute-start(bf16[2,256,512]{2,1,0:T(8,128)(2,1)S(1)} %collective-permute-done.4), channel_id=1, source_target_pairs={{0,56},{8,0},{16,8},{24,16},{32,24},{40,32},{48,40},{56,48},{1,57}... | collective-permute-start | bytes 1572872 | tf_op jit(solution)/shard_map/ppermute | solution.py:63
  58.1 35.4 %copy-start.12 = (bf16[32,128]{1,0:T(8,128)(2,1)S(1)}, bf16[32,128]{1,0:T(8,128)(2,1)}, u32[]{:S(2)}) copy-start(bf16[32,128]{1,0:T(8,128)(2,1)} %param.9) | copy-start | bytes 24580
  64.2 9.0 %collective-permute-start.12 = (bf16[256,512]{1,0:T(8,128)(2,1)S(1)}, bf16[256,512]{1,0:T(8,128)(2,1)S(1)}, u32[]{:S(2)}, u32[]{:S(2)}) collective-permute-start(bf16[256,512]{1,0:T(8,128)(2,1)S(1)} %slice_bitcast_fusion.6), channel_id=1, source_target_pairs={{0,56},{8,0},{16,8},{24,16},{32,24},{40,32},{48,40},{56,48},{1,57}... | collective-permute-start | bytes 786440 | tf_op jit(solution)/shard_map/ppermute | solution.py:71
  69.6 8.3 %collective-permute-start.11 = (bf16[256,512]{1,0:T(8,128)(2,1)S(1)}, bf16[256,512]{1,0:T(8,128)(2,1)S(1)}, u32[]{:S(2)}, u32[]{:S(2)}) collective-permute-start(bf16[256,512]{1,0:T(8,128)(2,1)S(1)} %slice_bitcast_fusion.7), channel_id=1, source_target_pairs={{0,8},{8,16},{16,24},{24,32},{32,40},{40,48},{48,56},{56,0},{1,9},... | collective-permute-start | bytes 786440 | tf_op jit(solution)/shard_map/ppermute | solution.py:70
  78.8 57.4 %collective-permute-start.13 = (bf16[8,2,256,512]{3,2,1,0:T(8,128)(2,1)}, bf16[8,2,256,512]{3,2,1,0:T(8,128)(2,1)}, u32[]{:S(2)}, u32[]{:S(2)}) collective-permute-start(bf16[8,2,256,512]{3,2,1,0:T(8,128)(2,1)} %fusion.71), channel_id=1, source_target_pairs={{0,4},{4,0},{1,5},{5,1},{2,6},{6,2},{3,7},{7,3},{8,12},{12,8},{9,1... | collective-permute-start | bytes 12582920 | tf_op jit(solution)/shard_map/ppermute | solution.py:74
  86.5 6.7 %collective-permute-start.7 = (bf16[127,512]{1,0:T(8,128)(2,1)S(1)}, bf16[127,512]{1,0:T(8,128)(2,1)S(1)}, u32[]{:S(2)}, u32[]{:S(2)}) collective-permute-start(bf16[127,512]{1,0:T(8,128)(2,1)S(1)} %slice.126), channel_id=1, source_target_pairs={{0,4},{4,8},{8,12},{12,16},{16,20},{20,24},{24,28},{28,32},{32,36}... | collective-permute-start | bytes 390152 | tf_op jit(solution)/shard_map/ppermute | solution.py:21
  106.8 10.4 %copy-start.10 = (bf16[256,512]{1,0:T(8,128)(2,1)S(1)}, bf16[256,512]{1,0:T(8,128)(2,1)}, u32[]{:S(2)}) copy-start(bf16[256,512]{1,0:T(8,128)(2,1)} %param.6) | copy-start | bytes 786436
  106.8 14.6 %copy-start.11 = (bf16[256,512]{1,0:T(8,128)(2,1)S(1)}, bf16[256,512]{1,0:T(8,128)(2,1)}, u32[]{:S(2)}) copy-start(bf16[256,512]{1,0:T(8,128)(2,1)} %param.10) | copy-start | bytes 786436
  117.4 7.9 %collective-permute-start.8 = (bf16[256,512]{0,1:T(8,128)(2,1)S(1)}, bf16[256,512]{0,1:T(8,128)(2,1)S(1)}, u32[]{:S(2)}, u32[]{:S(2)}) collective-permute-start(bf16[256,512]{0,1:T(8,128)(2,1)S(1)} %fusion.70), channel_id=1, source_target_pairs={{0,64},{64,128},{128,192},{192,256},{256,320},{320,384},{384,448},... | collective-permute-start | bytes 786440 | tf_op jit(solution)/shard_map/ppermute | solution.py:54
  125.3 19.2 %collective-permute-start.9 = (bf16[2,256,512]{1,2,0:T(8,128)(2,1)S(1)}, bf16[2,256,512]{1,2,0:T(8,128)(2,1)S(1)}, u32[]{:S(2)}, u32[]{:S(2)}) collective-permute-start(bf16[2,256,512]{1,2,0:T(8,128)(2,1)S(1)} %pad_maximum_fusion.1), channel_id=1, source_target_pairs={{0,8},{8,16},{16,24},{24,32},{32,40},{40,48},{48,56},{56,0},{1,9},... | collective-permute-start | bytes 1572872 | tf_op jit(solution)/shard_map/ppermute | solution.py:62
  127.3 17.3 %collective-permute-start.10 = (bf16[2,256,512]{1,2,0:T(8,128)(2,1)S(1)}, bf16[2,256,512]{1,2,0:T(8,128)(2,1)S(1)}, u32[]{:S(2)}, u32[]{:S(2)}) collective-permute-start(bf16[2,256,512]{1,2,0:T(8,128)(2,1)S(1)} %pad_maximum_fusion.1), channel_id=1, source_target_pairs={{0,56},{8,0},{16,8},{24,16},{32,24},{40,32},{48,40},{56,48},{1,57}... | collective-permute-start | bytes 1572872 | tf_op jit(solution)/shard_map/ppermute | solution.py:63
  151.0 14.4 %collective-permute-start.14 = (bf16[2,256,512]{1,2,0:T(8,128)(2,1)S(1)}, bf16[2,256,512]{1,2,0:T(8,128)(2,1)S(1)}, u32[]{:S(2)}, u32[]{:S(2)}) collective-permute-start(bf16[2,256,512]{1,2,0:T(8,128)(2,1)S(1)} %collective-permute-done.9), channel_id=1, source_target_pairs={{0,8},{8,16},{16,24},{24,32},{32,40},{40,48},{48,56},{56,0},{1,9},... | collective-permute-start | bytes 1572872 | tf_op jit(solution)/shard_map/ppermute | solution.py:62
  153.0 12.5 %collective-permute-start.15 = (bf16[2,256,512]{1,2,0:T(8,128)(2,1)S(1)}, bf16[2,256,512]{1,2,0:T(8,128)(2,1)S(1)}, u32[]{:S(2)}, u32[]{:S(2)}) collective-permute-start(bf16[2,256,512]{1,2,0:T(8,128)(2,1)S(1)} %collective-permute-done.10), channel_id=1, source_target_pairs={{0,56},{8,0},{16,8},{24,16},{32,24},{40,32},{48,40},{56,48},{1,57}... | collective-permute-start | bytes 1572872 | tf_op jit(solution)/shard_map/ppermute | solution.py:63
  171.9 14.8 %collective-permute-start.16 = (bf16[2,256,512]{1,2,0:T(8,128)(2,1)S(1)}, bf16[2,256,512]{1,2,0:T(8,128)(2,1)S(1)}, u32[]{:S(2)}, u32[]{:S(2)}) collective-permute-start(bf16[2,256,512]{1,2,0:T(8,128)(2,1)S(1)} %collective-permute-done.14), channel_id=1, source_target_pairs={{0,8},{8,16},{16,24},{24,32},{32,40},{40,48},{48,56},{56,0},{1,9},... | collective-permute-start | bytes 1572872 | tf_op jit(solution)/shard_map/ppermute | solution.py:62
  173.8 13.3 %collective-permute-start.17 = (bf16[2,256,512]{1,2,0:T(8,128)(2,1)S(1)}, bf16[2,256,512]{1,2,0:T(8,128)(2,1)S(1)}, u32[]{:S(2)}, u32[]{:S(2)}) collective-permute-start(bf16[2,256,512]{1,2,0:T(8,128)(2,1)S(1)} %collective-permute-done.15), channel_id=1, source_target_pairs={{0,56},{8,0},{16,8},{24,16},{32,24},{40,32},{48,40},{56,48},{1,57}... | collective-permute-start | bytes 1572872 | tf_op jit(solution)/shard_map/ppermute | solution.py:63
  187.2 7.8 %collective-permute-start.19 = (bf16[256,512]{0,1:T(8,128)(2,1)S(1)}, bf16[256,512]{0,1:T(8,128)(2,1)S(1)}, u32[]{:S(2)}, u32[]{:S(2)}) collective-permute-start(bf16[256,512]{0,1:T(8,128)(2,1)S(1)} %slice_bitcast_fusion.4), channel_id=1, source_target_pairs={{0,56},{8,0},{16,8},{24,16},{32,24},{40,32},{48,40},{56,48},{1,57}... | collective-permute-start | bytes 786440 | tf_op jit(solution)/shard_map/ppermute | solution.py:71
  191.1 8.3 %collective-permute-start.18 = (bf16[256,512]{0,1:T(8,128)(2,1)S(1)}, bf16[256,512]{0,1:T(8,128)(2,1)S(1)}, u32[]{:S(2)}, u32[]{:S(2)}) collective-permute-start(bf16[256,512]{0,1:T(8,128)(2,1)S(1)} %slice_bitcast_fusion.5), channel_id=1, source_target_pairs={{0,8},{8,16},{16,24},{24,32},{32,40},{40,48},{48,56},{56,0},{1,9},... | collective-permute-start | bytes 786440 | tf_op jit(solution)/shard_map/ppermute | solution.py:70
  200.3 31.5 %collective-permute-start.20 = (bf16[8,2,256,512]{2,3,1,0:T(8,128)(2,1)}, bf16[8,2,256,512]{2,3,1,0:T(8,128)(2,1)}, u32[]{:S(2)}, u32[]{:S(2)}) collective-permute-start(bf16[8,2,256,512]{2,3,1,0:T(8,128)(2,1)} %fusion.72), channel_id=1, source_target_pairs={{0,4},{4,0},{1,5},{5,1},{2,6},{6,2},{3,7},{7,3},{8,12},{12,8},{9,1... | collective-permute-start | bytes 12582920 | tf_op jit(solution)/shard_map/ppermute | solution.py:74
  213.0 7.2 %copy-start.3 = (f32[256,4096]{0,1:T(8,128)}, f32[256,4096]{0,1:T(8,128)S(1)}, u32[]{:S(2)}) copy-start(f32[256,4096]{0,1:T(8,128)S(1)} %get-tuple-element.92) | copy-start | bytes 12582916
  216.5 3.7 %copy-start.1 = (f32[256,4096]{0,1:T(8,128)}, f32[256,4096]{0,1:T(8,128)S(1)}, u32[]{:S(2)}) copy-start(f32[256,4096]{0,1:T(8,128)S(1)} %get-tuple-element.94) | copy-start | bytes 12582916
  238.3 5.3 %copy-start.4 = (bf16[8,2,256,512]{3,2,1,0:T(8,128)(2,1)S(1)}, bf16[8,2,256,512]{3,2,1,0:T(8,128)(2,1)}, u32[]{:S(2)}) copy-start(bf16[8,2,256,512]{3,2,1,0:T(8,128)(2,1)} %copy.43) | copy-start | bytes 12582916
  238.3 5.3 %copy-start.5 = (bf16[256,4096]{0,1:T(8,128)(2,1)S(1)}, bf16[256,4096]{0,1:T(8,128)(2,1)}, u32[]{:S(2)}) copy-start(bf16[256,4096]{0,1:T(8,128)(2,1)} %get-tuple-element.47) | copy-start | bytes 6291460
  240.8 3.6 %copy-start.2 = (f32[256,4096]{0,1:T(8,128)S(1)}, f32[256,4096]{0,1:T(8,128)}, u32[]{:S(2)}) copy-start(f32[256,4096]{0,1:T(8,128)} %copy-done.1) | copy-start | bytes 12582916
  244.5 2.9 %copy-start.7 = (bf16[256,4096]{0,1:T(8,128)(2,1)S(1)}, bf16[256,4096]{0,1:T(8,128)(2,1)}, u32[]{:S(2)}) copy-start(bf16[256,4096]{0,1:T(8,128)(2,1)} %get-tuple-element.52) | copy-start | bytes 6291460
  (2 other events, 4.2 us)
